TPU v7x, 32 devices: a whole 2x2x4 slice. The times are simulated.
32 devices in a mesh: dp: 4 (over y, core), freq: 8 (over z, x).
Axes of the slice: x: 2, y: 2, z: 4, core: 2. Of those that a mesh axis runs over, the one named last changes fastest.
Arguments:
- grad_parts: float32 [4, 27, 4, 65536], P('dp', None, None, 'freq'), may hold values from -12 to 12
- kernel: float32 [27, 262144], P(None, ('dp', 'freq')), may hold values from -4 to 4
Outputs:
- clipped: float32 [27, 262144], P(None, ('dp', 'freq'))
All inputs are finite; a program needn't handle non-finite values.
Results may differ from a plain program's by a relative error of at most 0.0005.
The roundings to bfloat16 on the way count: a program that leaves them out, or rounds other values in their place, can miss the bound.
Values may be sent and summed in bfloat16 or wider, within the bound.
No kernel may reach another device: no remote copies, remote signals or barrier semaphores. Data moves between devices by JAX's collectives and lax.ppermute only.
A program may use at most 64 MiB of HBM per device.

v0:
```python
import math
import jax
import jax.numpy as jnp
from jax import lax
from jax.sharding import PartitionSpec as P

C = 512
TAPS = 27
GT = 8
GH = 32
GW = 32
KD = 2
CLIP = 0.25
HIGH = lax.Precision.HIGHEST


def tap_phases(freq_ids, stride):
    flat_index = freq_ids * stride
    freq_time = flat_index // (GH * GW)
    freq_row = flat_index // GW % GH
    freq_col = flat_index % GW
    taps = jnp.arange(TAPS, dtype=jnp.int32)
    off_time = taps // 9 - 1
    off_row = taps // 3 % 3 - 1
    off_col = taps % 3 - 1
    period = GT * GH * GW
    turns = (
        freq_time[:, None] * off_time[None, :] * (GH * GW)
        + freq_row[:, None] * off_row[None, :] * (GT * GW)
        + freq_col[:, None] * off_col[None, :] * (GT * GH)
    ) % period
    angle = turns.astype(jnp.float32) * (2.0 * math.pi / period)
    return (jnp.cos(angle), jnp.sin(angle))


def clip_factor(local_square):
    summed = lax.psum(local_square, ("dp", "freq"))
    return jnp.minimum(1.0, CLIP * math.sqrt(TAPS * C * C) / jnp.sqrt(summed + 1e-06))


def spectrum(field, cosine, sine_rows):
    real_spec = jnp.dot(cosine, field, precision=HIGH)
    imag_spec = -jnp.dot(sine_rows, field, precision=HIGH)
    return jnp.stack([real_spec, imag_spec], axis=1)


def taps_back(polar_part, cosine, sine_rows):
    values = polar_part.astype(jnp.float32)
    summed = jnp.dot(cosine.T, values[:, 0], precision=HIGH)
    return summed - jnp.dot(sine_rows.T, values[:, 1], precision=HIGH)


def polar_step(spectra):
    width = spectra.shape[-1]
    mean_square = jnp.mean(jnp.square(spectra.astype(jnp.float32)), axis=(1, 2, 3), keepdims=True)
    spread = math.sqrt(8.0 * width)
    scaled = (
        spectra.astype(jnp.float32) * (0.75 / (spread * jnp.sqrt(mean_square + 1e-06)))
    ).astype(jnp.bfloat16)
    real_part = scaled[:, 0]
    imag_part = scaled[:, 1]
    stacked = jnp.concatenate([real_part, imag_part], axis=1)
    turned = jnp.concatenate([imag_part, -real_part], axis=1)
    gram = jnp.einsum(
        "nri,nrj->nij",
        stacked,
        jnp.concatenate([stacked, turned], axis=2),
        preferred_element_type=jnp.float32,
    ).astype(jnp.bfloat16)
    gram_real = gram[:, :, :width]
    gram_imag = gram[:, :, width:]
    blocked = jnp.concatenate([gram, jnp.concatenate([-gram_imag, gram_real], axis=2)], axis=1)
    side = jnp.concatenate([real_part, imag_part], axis=2)
    product = jnp.einsum("nij,njk->nik", side, blocked, preferred_element_type=jnp.float32)
    result = (1.5 * side.astype(jnp.float32) - 0.5 * product).astype(jnp.bfloat16)
    return jnp.stack([result[:, :, :width], result[:, :, width:]], axis=1)


def on_device(grad_parts, kernel):
    devices_dp = lax.axis_size("dp")
    devices_freq = lax.axis_size("freq")
    total_freq = KD * devices_dp * devices_freq
    stride = GT * GH * GW // total_freq
    scale_out = math.sqrt(C / total_freq)
    own_width = kernel.shape[1]
    gradient = lax.psum_scatter(grad_parts[0], "dp", scatter_dimension=1, tiled=True).reshape(
        TAPS, own_width
    )
    local_square = jnp.sum(gradient * gradient)
    kernel_all, gradient_all = (kernel, gradient)
    freq_ids = jnp.arange(total_freq, dtype=jnp.int32)
    cosine, sine_rows = tap_phases(freq_ids, stride)
    factor = clip_factor(local_square)
    spectra = spectrum(kernel_all - factor * gradient_all, cosine, sine_rows)
    spectra = spectra.astype(jnp.bfloat16)
    count, row_width = (spectra.shape[0], spectra.shape[2])
    whole = lax.all_to_all(
        lax.all_to_all(
            spectra.reshape(count, 2, 1, 1, row_width),
            "dp",
            split_axis=0,
            concat_axis=2,
            tiled=True,
        ),
        "freq",
        split_axis=0,
        concat_axis=3,
        tiled=True,
    )
    polar_part = polar_step(whole.reshape(KD, 2, C, C))
    returned = lax.all_to_all(
        lax.all_to_all(
            polar_part.reshape(KD, 2, devices_dp, devices_freq, row_width),
            "dp",
            split_axis=2,
            concat_axis=0,
            tiled=True,
        ),
        "freq",
        split_axis=3,
        concat_axis=0,
        tiled=True,
    )
    position = jnp.arange(total_freq, dtype=jnp.int32)
    source_freq = position // (devices_dp * KD)
    source_dp = position // KD % devices_dp
    member = position % KD
    back_ids = source_dp * (devices_freq * KD) + source_freq * KD + member
    back_cos, back_sin = tap_phases(back_ids, stride)
    return taps_back(returned.reshape(count, 2, row_width), back_cos, back_sin) * scale_out


def solution(mesh):
    return jax.shard_map(
        on_device,
        mesh=mesh,
        in_specs=(P("dp", None, None, "freq"), P(None, ("dp", "freq"))),
        out_specs=P(None, ("dp", "freq")),
        check_vma=False,
    )
```

profile of v0, /device:TPU:0, one launch (start us, length us, event | category | flops | bytes accessed | tf_op | source)
XLA Modules:
  0.0 307.9 jit_solution(1594015570563499403)
XLA Ops:
  6.5 0.0 reduce-scatter.2.cloned.1.call-start
  6.5 6.0 %copy.47 = f32[1,27,4,8192]{3,1,2,0:T(8,128)} copy(f32[1,27,4,8192]{3,2,1,0:T(4,128)} %param.2) | data formatting | bytes 7077888 | tf_op args[0]
  12.5 0.0 copy-start.1
  12.5 0.0 reduce-scatter.2.cloned.1.call-update
  12.6 47.3 %reduce-scatter.2.cloned.1.call-done = f32[27,1,8192]{2,0,1:T(8,128)} async-done(((f32[27,4,8192]{2,0,1:T(8,128)}), f32[27,1,8192]{2,0,1:T(8,128)}) %reduce-scatter.2.cloned.1.call-update) | async-done | bytes 884752 | tf_op jit(solution)/shard_map/reduce_scatter | solution.py:86
  59.9 0.0 copy-start
  59.9 2.2 multiply_reduce_fusion.1
  62.1 39.5 %psum.7 = f32[]{:T(128)} all-reduce(f32[]{:T(128)} %multiply_reduce_fusion.1), channel_id=1, replica_groups=mesh['dp'=4,'freq'=8] {'dp','freq'}, use_global_device_ids=true, to_apply=%region_2.3 | all-reduce | flops 1 | bytes 8 | tf_op jit(solution)/shard_map/psum | solution.py:37
  102.3 0.0 copy-done.1
  102.3 3.2 %fusion.2 = bf16[64,1,1,1,8192]{4,0,3,2,1:T(8,128)(2,1)S(1)} fusion(f32[27,8192]{1,0:T(8,128)S(1)} %copy-done.1, f32[27,1,8192]{2,0,1:T(8,128)} %reduce-scatter.2.cloned.1.call-done, f32[]{:T(128)S(6)} %min_shard_map.3, s32[64]{0:T(128)S(1)} %get-tuple-element.11, s32[64]{0:T(128)S(1)} %get-tuple-element.12, s32[64]{0:T(128)S(1)} %and_select_fusion.3, ...), kind=kOutput, calls=%fused_computation.4 | convolution fusion | flops 171396544 | bytes 2819144 | tf_op jit(solution)/shard_map/dot_general | solution.py:43
  105.6 0.0 copy-done
  105.6 2.0 fusion.1
  107.6 0.2 pad_maximum_fusion
  107.8 2.2 copy.32
  110.0 29.2 %all_to_all.60 = bf16[64,2,1,1,8192]{4,1,3,2,0:T(2,128)(2,1)S(1)} all-to-all(bf16[64,2,1,1,8192]{4,1,3,2,0:T(2,128)(2,1)S(1)} %copy.32), channel_id=1, replica_groups=mesh['dp'=4,'freq'=8] {'dp'}, dimensions={0} | all-to-all | bytes 4194304 | tf_op jit(solution)/shard_map/all_to_all | solution.py:98
  139.2 1.2 copy.33
  140.4 1.6 copy.34
  142.0 52.3 %all_to_all.61 = bf16[16,2,4,1,8192]{4,2,1,3,0:T(4,128)(2,1)S(1)} all-to-all(bf16[16,2,4,1,8192]{4,2,1,3,0:T(4,128)(2,1)S(1)} %copy.34), channel_id=1, replica_groups=mesh['dp'=4,'freq'=8] {'freq'}, dimensions={0} | all-to-all | bytes 4194304 | tf_op jit(solution)/shard_map/all_to_all | solution.py:97
  194.3 1.2 multiply_reduce_fusion
  195.6 0.1 reduce_sum.27
  195.7 3.2 %copy.46 = f32[8,2,2,4,1,8192]{5,0,3,1,2,4:T(8,128)} copy(bf16[8,2,2,4,1,8192]{5,3,2,1,0,4:T(4,128)(2,1)S(1)} %bitcast.49) | data formatting | bytes 6291456 | tf_op jit(solution)/shard_map/convert_element_type | solution.py:58
  198.8 5.0 %reshape.259 = f32[2,2,512,512]{3,2,0,1:T(8,128)} reshape(f32[2,2,4,8,1,8192]{5,3,2,0,1,4:T(8,128)} %bitcast.50) | data formatting | bytes 8388608 | tf_op jit(solution)/shard_map/convert_element_type | solution.py:58
  203.8 2.8 multiply_convert_fusion
  206.6 0.1 fusion.83
  206.7 0.1 slice_bitcast_fusion.5
  206.9 2.6 fusion.23
  209.5 0.1 slice_negate_fusion
  209.6 2.6 subtract_convert_fusion
  212.2 0.2 fusion.84
  212.4 0.5 stack.21
  212.9 0.5 stack.22
  213.5 0.2 pad_maximum_fusion.2
  213.7 0.2 copy.42
  213.9 28.2 %all_to_all.62 = bf16[2,2,4,8,8192]{4,3,1,0,2:T(8,128)(2,1)S(1)} all-to-all(bf16[2,2,4,8,8192]{4,3,1,0,2:T(8,128)(2,1)S(1)} %copy.42), channel_id=1, replica_groups=mesh['dp'=4,'freq'=8] {'dp'}, dimensions={2} | all-to-all | bytes 4194304 | tf_op jit(solution)/shard_map/all_to_all | solution.py:112
  242.0 3.5 %copy.39 = bf16[8,2,1,8,8192]{4,1,0,2,3:T(2,128)(2,1)} copy(bf16[8,2,1,8,8192]{4,3,1,0,2:T(8,128)(2,1)S(1)} %bitcast.55) | data formatting | bytes 4194304 | tf_op jit(solution)/shard_map/all_to_all | solution.py:112
  245.6 3.6 %all-to-all-start.3 = ((bf16[8,2,1,8,8192]{4,1,0,2,3:T(2,128)(2,1)}), bf16[8,2,1,8,8192]{4,1,0,2,3:T(2,128)(2,1)S(1)}, u32[]{:S(2)}, u32[]{:S(2)}) async-start(bf16[8,2,1,8,8192]{4,1,0,2,3:T(2,128)(2,1)} %copy.39), calls=%async_computation.4 | async-start | bytes 4194304 | tf_op jit(solution)/shard_map/all_to_all | solution.py:111
  249.2 48.0 %all-to-all-done.3 = bf16[8,2,1,8,8192]{4,1,0,2,3:T(2,128)(2,1)S(1)} async-done(((bf16[8,2,1,8,8192]{4,1,0,2,3:T(2,128)(2,1)}), bf16[8,2,1,8,8192]{4,1,0,2,3:T(2,128)(2,1)S(1)}, u32[]{:S(2)}, u32[]{:S(2)}) %all-to-all-start.3) | async-done | bytes 2097184 | tf_op jit(solution)/shard_map/all_to_all | solution.py:111
  297.2 1.2 copy.48
  298.4 0.8 fusion.28
  299.2 1.8 fusion.3
  (8 shorter events, 0.1 us)
Async XLA Ops:
  6.5 53.4 %reduce-scatter.2.cloned.1.call-start = ((), (), s32[]{:S(2)}) async-start(), calls=%async_computation.5 | async-start | bytes 5242880 | tf_op jit(solution)/shard_map/reduce_scatter | solution.py:86
  12.5 89.8 %copy-start.1 = (f32[27,8192]{1,0:T(8,128)S(1)}, f32[27,8192]{1,0:T(8,128)}, u32[]{:S(2)}) copy-start(f32[27,8192]{1,0:T(8,128)} %param.3) | copy-start | bytes 2654212
  59.9 45.7 %copy-start = (f32[27,1,8192]{2,0,1:T(8,128)S(1)}, f32[27,1,8192]{2,0,1:T(8,128)}, u32[]{:S(2)}) copy-start(f32[27,1,8192]{2,0,1:T(8,128)} %reduce-scatter.2.cloned.1.call-done) | copy-start | bytes 2654212
  245.6 51.7 %all-to-all-start.3 = ((bf16[8,2,1,8,8192]{4,1,0,2,3:T(2,128)(2,1)}), bf16[8,2,1,8,8192]{4,1,0,2,3:T(2,128)(2,1)S(1)}, u32[]{:S(2)}, u32[]{:S(2)}) async-start(bf16[8,2,1,8,8192]{4,1,0,2,3:T(2,128)(2,1)} %copy.39), calls=%async_computation.4 | async-start | bytes 4194304 | tf_op jit(solution)/shard_map/all_to_all | solution.py:111
Sparse Core Ops, SparseCore 0:
  12.7 47.2 reduce-scatter.1
where the time goes:
time: 308 us
  blocking collectives  149 us (48%)
  waiting for transfers between devices  95.4 us (31%)
  local copies, waits for them, and re-layouts  25.4 us (8%)
  between operations  14.3 us (5%)
  matrix products  13 us (4%)
  other arithmetic  6.98 us (2%)
  starting transfers between devices  3.6 us (1%)
    all_to_all x1, blocking collectives, on_device(): lax.all_to_all(lax.all_to_all(spectra.reshape(count, 2, 1, 1, row_width),...  52.3 us
    all_to_all x1, waiting for transfers between devices, on_device(): lax.all_to_all(lax.all_to_all(polar_part.reshape(KD, 2, devices_dp, devic...  48 us
    reduce_scatter x1, waiting for transfers between devices, on_device(): lax.psum_scatter(grad_parts[0], 'dp', scatter_dimension=1, tiled=True)  47.3 us
    psum x1, blocking collectives, clip_factor(): summed = lax.psum(local_square, ('dp', 'freq'))  39.5 us
    all_to_all x1, blocking collectives, on_device(): lax.all_to_all(spectra.reshape(count, 2, 1, 1, row_width), 'dp', split_ax...  29.2 us
    all_to_all x1, blocking collectives, on_device(): lax.all_to_all(polar_part.reshape(KD, 2, devices_dp, devices_freq, row_wi...  28.2 us
    convert_element_type x2, local copies, waits for them, and re-layouts, polar_step(): spectra.astype(jnp.float32)  8.14 us
  transfers between devices with their start and end apart: 2, of which 2 were waited for; matrix products, arithmetic and copies ran while one was open for 0% of the time, Pallas kernels for 0%

commit v1 on v0

--- a/solution.py
+++ b/solution.py
@@ -12,6 +12,28 @@
 KD = 2
 CLIP = 0.25
 HIGH = lax.Precision.HIGHEST
+
+
+def cut_along(array, dim, count):
+    before, after = (array.shape[:dim], array.shape[dim + 1 :])
+    return jnp.moveaxis(array.reshape(*before, count, -1, *after), dim, 0)
+
+
+def in_order(parts, dim):
+    parts = jnp.moveaxis(parts, 0, dim)
+    lengths = parts.shape
+    return parts.reshape(*lengths[:dim], lengths[dim] * lengths[dim + 1], *lengths[dim + 2 :])
+
+
+def swapped_with_each(x, axis, split_dim, concat_dim):
+    peers, here = (lax.axis_size(axis), lax.axis_index(axis))
+    pieces = cut_along(x, split_dim, peers)
+    outs = [pieces[here]]
+    for step in range(1, peers):
+        sent = pieces[here ^ step]
+        outs.append(lax.ppermute(sent, axis, [(i, i ^ step) for i in range(peers)]))
+    pieces = jnp.stack(outs)[here ^ jnp.arange(peers)]
+    return in_order(pieces, concat_dim)
 
 
 def tap_phases(freq_ids, stride):
@@ -94,7 +116,7 @@
     spectra = spectrum(kernel_all - factor * gradient_all, cosine, sine_rows)
     spectra = spectra.astype(jnp.bfloat16)
     count, row_width = (spectra.shape[0], spectra.shape[2])
-    whole = lax.all_to_all(
+    whole = swapped_with_each(
         lax.all_to_all(
             spectra.reshape(count, 2, 1, 1, row_width),
             "dp",
@@ -103,9 +125,8 @@
             tiled=True,
         ),
         "freq",
-        split_axis=0,
-        concat_axis=3,
-        tiled=True,
+        0,
+        3,
     )
     polar_part = polar_step(whole.reshape(KD, 2, C, C))
     returned = lax.all_to_all(

time: 308 us -> 318 us (1.032)
  blocking collectives: 149 us -> 67.7 us
  waiting for transfers between devices: 95.4 us -> 159 us
  starting transfers between devices: 3.6 us -> 20.9 us
  local copies, waits for them, and re-layouts: 25.4 us -> 34.9 us
    all_to_all x2 -> x0, blocking collectives: 81.6 us -> none  [the longest x1 52.3 us: on_device(): lax.all_to_all(lax.all_to_all(spectra.reshape(count, 2, 1, 1, row_width),...]
    ppermute x0 -> x7, waiting for transfers between devices: none -> 37.9 us  [swapped_with_each(): outs.append(lax.ppermute(sent, axis, [(i, i ^ step) for i in range(peers)]))]
    all_to_all x0 -> x1, waiting for transfers between devices: none -> 25.6 us  [on_device(): lax.all_to_all(spectra.reshape(count, 2, 1, 1, row_width), 'dp', split_ax...]
    ppermute x0 -> x7, starting transfers between devices: none -> 13.5 us  [swapped_with_each(): outs.append(lax.ppermute(sent, axis, [(i, i ^ step) for i in range(peers)]))]
    gather x0 -> x1, local copies, waits for them, and re-layouts: none -> 3.95 us  [swapped_with_each(): pieces = jnp.stack(outs)[here ^ jnp.arange(peers)]]
    all_to_all x0 -> x1, starting transfers between devices: none -> 3.79 us  [on_device(): lax.all_to_all(spectra.reshape(count, 2, 1, 1, row_width), 'dp', split_ax...]
    unnamed x5 -> x13, local copies, waits for them, and re-layouts: 5.99 us -> 8.05 us
  transfers between devices with their start and end apart: 2 -> 10, of which waited for: 2 -> 6; matrix products, arithmetic and copies ran while one was open for 0% -> 0% of each run, Pallas kernels for 0% -> 0%
where the time goes in v1:
time: 318 us; the launch traced here: 317 us
  waiting for transfers between devices  159 us (50%)
  blocking collectives  67.7 us (21%)
  local copies, waits for them, and re-layouts  34.9 us (11%)
  starting transfers between devices  20.9 us (7%)
  between operations  14.4 us (5%)
  matrix products  13 us (4%)
  other arithmetic  7.42 us (2%)
    all_to_all x1, waiting for transfers between devices, on_device(): lax.all_to_all(lax.all_to_all(polar_part.reshape(KD, 2, devices_dp, devic...  48 us
    reduce_scatter x1, waiting for transfers between devices, on_device(): lax.psum_scatter(grad_parts[0], 'dp', scatter_dimension=1, tiled=True)  47.3 us
    psum x1, blocking collectives, clip_factor(): summed = lax.psum(local_square, ('dp', 'freq'))  39.5 us
    ppermute x7, waiting for transfers between devices, swapped_with_each(): outs.append(lax.ppermute(sent, axis, [(i, i ^ step) for i in range(peers)]))  37.9 us
    all_to_all x1, blocking collectives, on_device(): lax.all_to_all(polar_part.reshape(KD, 2, devices_dp, devices_freq, row_wi...  28.2 us
    all_to_all x1, waiting for transfers between devices, on_device(): lax.all_to_all(spectra.reshape(count, 2, 1, 1, row_width), 'dp', split_ax...  25.6 us
    ppermute x7, starting transfers between devices, swapped_with_each(): outs.append(lax.ppermute(sent, axis, [(i, i ^ step) for i in range(peers)]))  13.5 us
    convert_element_type x2, local copies, waits for them, and re-layouts, polar_step(): spectra.astype(jnp.float32)  9.35 us
  transfers between devices with their start and end apart: 10, of which 6 were waited for; matrix products, arithmetic and copies ran while one was open for 0% of the time, Pallas kernels for 0%

profile of v1, /device:TPU:0, one launch (start us, length us, event | category | flops | bytes accessed | tf_op | source)
XLA Modules:
  0.0 317.2 jit_solution(2661396727386740311)
XLA Ops:
  6.5 6.0 %copy.45 = f32[1,27,4,8192]{3,1,2,0:T(8,128)} copy(f32[1,27,4,8192]{3,2,1,0:T(4,128)} %param.2) | data formatting | bytes 7077888 | tf_op args[0]
  12.6 47.3 %reduce-scatter.2.cloned.1.call-done = f32[27,1,8192]{2,0,1:T(8,128)} async-done(((f32[27,4,8192]{2,0,1:T(8,128)}), f32[27,1,8192]{2,0,1:T(8,128)}) %reduce-scatter.2.cloned.1.call-update) | async-done | bytes 884752 | tf_op jit(solution)/shard_map/reduce_scatter | solution.py:108
  60.0 2.2 multiply_reduce_fusion
  62.1 39.5 %psum.7 = f32[]{:T(128)} all-reduce(f32[]{:T(128)} %multiply_reduce_fusion), channel_id=1, replica_groups=mesh['dp'=4,'freq'=8] {'dp','freq'}, use_global_device_ids=true, to_apply=%region_2.3 | all-reduce | flops 1 | bytes 8 | tf_op jit(solution)/shard_map/psum | solution.py:59
  102.4 3.2 %fusion.2 = bf16[64,1,1,1,8192]{4,0,3,2,1:T(8,128)(2,1)S(1)} fusion(f32[27,8192]{1,0:T(8,128)S(1)} %copy-done.1, f32[27,1,8192]{2,0,1:T(8,128)} %reduce-scatter.2.cloned.1.call-done, f32[]{:T(128)S(6)} %min_shard_map.3, s32[64]{0:T(128)S(1)} %get-tuple-element.19, s32[64]{0:T(128)S(1)} %get-tuple-element.20, s32[64]{0:T(128)S(1)} %and_select_fusion.3, ...), kind=kOutput, calls=%fused_computation.5 | convolution fusion | flops 171396544 | bytes 2819144 | tf_op jit(solution)/shard_map/dot_general | solution.py:65
  105.6 2.0 fusion.1
  107.6 0.2 pad_maximum_fusion
  107.8 3.5 %copy.32 = bf16[64,2,1,1,8192]{4,1,3,2,0:T(2,128)(2,1)} copy(bf16[64,2,1,1,8192]{4,0,3,2,1:T(8,128)(2,1)S(1)} %pad_maximum_fusion) | data formatting | bytes 4194304 | tf_op jit(solution)/shard_map/stack | solution.py:66
  111.3 3.8 %all-to-all-start = ((bf16[64,2,1,1,8192]{4,1,3,2,0:T(2,128)(2,1)}), bf16[64,2,1,1,8192]{4,1,3,2,0:T(2,128)(2,1)S(1)}, u32[]{:S(2)}, u32[]{:S(2)}) async-start(bf16[64,2,1,1,8192]{4,1,3,2,0:T(2,128)(2,1)} %copy.32), calls=%async_computation.1 | async-start | bytes 4194304 | tf_op jit(solution)/shard_map/all_to_all | solution.py:120
  115.1 25.6 %all-to-all-done = bf16[64,2,1,1,8192]{4,1,3,2,0:T(2,128)(2,1)S(1)} async-done(((bf16[64,2,1,1,8192]{4,1,3,2,0:T(2,128)(2,1)}), bf16[64,2,1,1,8192]{4,1,3,2,0:T(2,128)(2,1)S(1)}, u32[]{:S(2)}, u32[]{:S(2)}) %all-to-all-start) | async-done | bytes 2097184 | tf_op jit(solution)/shard_map/all_to_all | solution.py:120
  140.7 1.2 copy.33
  141.9 1.6 copy.34
  143.5 0.9 dynamic-slice_bitcast_fusion
  144.4 2.2 collective-permute-start
  146.6 1.8 collective-permute-start.6
  148.4 1.6 collective-permute-start.5
  150.0 1.9 collective-permute-start.4
  151.9 2.4 collective-permute-start.3
  154.3 3.6 %collective-permute-done = bf16[2,2,4,1,8192]{4,2,1,0,3:T(4,128)(2,1)S(1)} collective-permute-done((bf16[2,2,4,1,8192]{4,2,1,0,3:T(4,128)(2,1)S(1)}, bf16[2,2,4,1,8192]{4,2,1,0,3:T(4,128)(2,1)S(1)}, u32[]{:S(2)}, u32[]{:S(2)}) %collective-permute-start) | collective-permute-done | bytes 262176 | tf_op jit(solution)/shard_map/ppermute | solution.py:34
  158.1 18.2 %collective-permute-done.1 = bf16[2,2,4,1,8192]{4,2,1,0,3:T(4,128)(2,1)S(1)} collective-permute-done((bf16[2,2,4,1,8192]{4,2,1,0,3:T(4,128)(2,1)S(1)}, bf16[2,2,4,1,8192]{4,2,1,0,3:T(4,128)(2,1)S(1)}, u32[]{:S(2)}, u32[]{:S(2)}) %collective-permute-start.1) | collective-permute-done | bytes 262176 | tf_op jit(solution)/shard_map/ppermute | solution.py:34
  176.3 3.6 %collective-permute-start.2 = (bf16[2,2,4,1,8192]{4,2,1,0,3:T(4,128)(2,1)S(1)}, bf16[2,2,4,1,8192]{4,2,1,0,3:T(4,128)(2,1)S(1)}, u32[]{:S(2)}, u32[]{:S(2)}) collective-permute-start(bf16[2,2,4,1,8192]{4,2,1,0,3:T(4,128)(2,1)S(1)} %get-tuple-element.15), channel_id=1, source_target_pairs={{0,3},{1,2},{2,1},{3,0},{4,7},{5,6},{6,5},{7,4},{8,11},{9,10},{10,... | collective-permute-start | bytes 786440 | tf_op jit(solution)/shard_map/ppermute | solution.py:34
  180.0 16.1 %collective-permute-done.2 = bf16[2,2,4,1,8192]{4,2,1,0,3:T(4,128)(2,1)S(1)} collective-permute-done((bf16[2,2,4,1,8192]{4,2,1,0,3:T(4,128)(2,1)S(1)}, bf16[2,2,4,1,8192]{4,2,1,0,3:T(4,128)(2,1)S(1)}, u32[]{:S(2)}, u32[]{:S(2)}) %collective-permute-start.2) | collective-permute-done | bytes 262176 | tf_op jit(solution)/shard_map/ppermute | solution.py:34
  196.2 0.1 bitcast_dynamic-update-slice_fusion.3
  196.5 0.1 bitcast_dynamic-update-slice_fusion.1
  196.6 0.1 bitcast_dynamic-update-slice_fusion
  196.7 1.3 copy-done.2
  198.1 4.0 %gather_fusion = bf16[8,2,2,4,8192]{4,3,2,1,0:T(4,128)(2,1)S(1)} fusion(bf16[8,2,2,4,8192]{4,3,2,1,0:T(4,128)(2,1)} %bitcast.86, s32[1024]{0:T(1024)S(1)} %pad_clamp_fusion), kind=kCustom, calls=%fused_computation | custom fusion | bytes 4194336 | tf_op jit(solution)/shard_map/gather | solution.py:35
  202.0 1.2 fusion.4
  203.2 0.5 convert_bitcast_fusion
  203.8 4.4 %copy.35 = f32[2,2,4,8,1,8192]{5,3,2,0,1,4:T(8,128)} copy(f32[2,2,4,8,1,8192]{5,2,1,0,3,4:T(4,128)S(1)} %convert_bitcast_fusion) | data formatting | bytes 8388608 | tf_op jit(solution)/shard_map/convert_element_type | solution.py:80
  208.1 5.0 %reshape.272 = f32[2,2,512,512]{3,2,0,1:T(8,128)} reshape(f32[2,2,4,8,1,8192]{5,3,2,0,1,4:T(8,128)} %copy.35) | data formatting | bytes 8388608 | tf_op jit(solution)/shard_map/convert_element_type | solution.py:80
  213.1 2.8 multiply_convert_fusion
  216.0 0.1 slice_bitcast_fusion.5
  216.1 2.6 fusion.24
  218.8 0.1 slice_negate_fusion
  218.9 2.6 subtract_convert_fusion
  221.5 0.2 fusion.86
  221.7 0.5 stack.53
  222.2 0.5 stack.54
  222.8 0.2 pad_maximum_fusion.2
  223.0 0.2 copy.42
  223.2 28.2 %all_to_all.48 = bf16[2,2,4,8,8192]{4,3,1,0,2:T(8,128)(2,1)S(1)} all-to-all(bf16[2,2,4,8,8192]{4,3,1,0,2:T(8,128)(2,1)S(1)} %copy.42), channel_id=1, replica_groups=mesh['dp'=4,'freq'=8] {'dp'}, dimensions={2} | all-to-all | bytes 4194304 | tf_op jit(solution)/shard_map/all_to_all | solution.py:133
  251.3 3.5 %copy.39 = bf16[8,2,1,8,8192]{4,1,0,2,3:T(2,128)(2,1)} copy(bf16[8,2,1,8,8192]{4,3,1,0,2:T(8,128)(2,1)S(1)} %bitcast.85) | data formatting | bytes 4194304 | tf_op jit(solution)/shard_map/all_to_all | solution.py:133
  254.8 3.6 %all-to-all-start.2 = ((bf16[8,2,1,8,8192]{4,1,0,2,3:T(2,128)(2,1)}), bf16[8,2,1,8,8192]{4,1,0,2,3:T(2,128)(2,1)S(1)}, u32[]{:S(2)}, u32[]{:S(2)}) async-start(bf16[8,2,1,8,8192]{4,1,0,2,3:T(2,128)(2,1)} %copy.39), calls=%async_computation.3 | async-start | bytes 4194304 | tf_op jit(solution)/shard_map/all_to_all | solution.py:132
  258.5 48.0 %all-to-all-done.2 = bf16[8,2,1,8,8192]{4,1,0,2,3:T(2,128)(2,1)S(1)} async-done(((bf16[8,2,1,8,8192]{4,1,0,2,3:T(2,128)(2,1)}), bf16[8,2,1,8,8192]{4,1,0,2,3:T(2,128)(2,1)S(1)}, u32[]{:S(2)}, u32[]{:S(2)}) %all-to-all-start.2) | async-done | bytes 2097184 | tf_op jit(solution)/shard_map/all_to_all | solution.py:132
  306.5 1.2 copy.46
  307.7 0.8 fusion.29
  308.5 1.8 fusion.3
  (26 shorter events, 0.7 us)
Async XLA Ops:
  6.5 53.4 %reduce-scatter.2.cloned.1.call-start = ((), (), s32[]{:S(2)}) async-start(), calls=%async_computation.4 | async-start | bytes 5242880 | tf_op jit(solution)/shard_map/reduce_scatter | solution.py:108
  12.5 89.8 %copy-start.1 = (f32[27,8192]{1,0:T(8,128)S(1)}, f32[27,8192]{1,0:T(8,128)}, u32[]{:S(2)}) copy-start(f32[27,8192]{1,0:T(8,128)} %param.3) | copy-start | bytes 2654212
  59.9 45.6 %copy-start = (f32[27,1,8192]{2,0,1:T(8,128)S(1)}, f32[27,1,8192]{2,0,1:T(8,128)}, u32[]{:S(2)}) copy-start(f32[27,1,8192]{2,0,1:T(8,128)} %reduce-scatter.2.cloned.1.call-done) | copy-start | bytes 2654212
  111.3 29.4 %all-to-all-start = ((bf16[64,2,1,1,8192]{4,1,3,2,0:T(2,128)(2,1)}), bf16[64,2,1,1,8192]{4,1,3,2,0:T(2,128)(2,1)S(1)}, u32[]{:S(2)}, u32[]{:S(2)}) async-start(bf16[64,2,1,1,8192]{4,1,3,2,0:T(2,128)(2,1)} %copy.32), calls=%async_computation.1 | async-start | bytes 4194304 | tf_op jit(solution)/shard_map/all_to_all | solution.py:120
  144.4 13.6 %collective-permute-start = (bf16[2,2,4,1,8192]{4,2,1,0,3:T(4,128)(2,1)S(1)}, bf16[2,2,4,1,8192]{4,2,1,0,3:T(4,128)(2,1)S(1)}, u32[]{:S(2)}, u32[]{:S(2)}) collective-permute-start(bf16[2,2,4,1,8192]{4,2,1,0,3:T(4,128)(2,1)S(1)} %get-tuple-element.17), channel_id=1, source_target_pairs={{0,1},{1,0},{2,3},{3,2},{4,5},{5,4},{6,7},{7,6},{8,9},{9,8},{10,11... | collective-permute-start | bytes 786440 | tf_op jit(solution)/shard_map/ppermute | solution.py:34
  146.6 50.0 %collective-permute-start.6 = (bf16[2,2,4,1,8192]{4,2,1,0,3:T(4,128)(2,1)S(1)}, bf16[2,2,4,1,8192]{4,2,1,0,3:T(4,128)(2,1)S(1)}, u32[]{:S(2)}, u32[]{:S(2)}) collective-permute-start(bf16[2,2,4,1,8192]{4,2,1,0,3:T(4,128)(2,1)S(1)} %get-tuple-element.11), channel_id=1, source_target_pairs={{0,7},{1,6},{2,5},{3,4},{4,3},{5,2},{6,1},{7,0},{8,15},{9,14},{10,... | collective-permute-start | bytes 786440 | tf_op jit(solution)/shard_map/ppermute | solution.py:34
  148.4 48.1 %collective-permute-start.5 = (bf16[2,2,4,1,8192]{4,2,1,0,3:T(4,128)(2,1)S(1)}, bf16[2,2,4,1,8192]{4,2,1,0,3:T(4,128)(2,1)S(1)}, u32[]{:S(2)}, u32[]{:S(2)}) collective-permute-start(bf16[2,2,4,1,8192]{4,2,1,0,3:T(4,128)(2,1)S(1)} %get-tuple-element.12), channel_id=1, source_target_pairs={{0,6},{1,7},{2,4},{3,5},{4,2},{5,3},{6,0},{7,1},{8,14},{9,15},{10,... | collective-permute-start | bytes 786440 | tf_op jit(solution)/shard_map/ppermute | solution.py:34
  150.0 46.4 %collective-permute-start.4 = (bf16[2,2,4,1,8192]{4,2,1,0,3:T(4,128)(2,1)S(1)}, bf16[2,2,4,1,8192]{4,2,1,0,3:T(4,128)(2,1)S(1)}, u32[]{:S(2)}, u32[]{:S(2)}) collective-permute-start(bf16[2,2,4,1,8192]{4,2,1,0,3:T(4,128)(2,1)S(1)} %get-tuple-element.13), channel_id=1, source_target_pairs={{0,5},{1,4},{2,7},{3,6},{4,1},{5,0},{6,3},{7,2},{8,13},{9,12},{10,... | collective-permute-start | bytes 786440 | tf_op jit(solution)/shard_map/ppermute | solution.py:34
  151.9 44.3 %collective-permute-start.3 = (bf16[2,2,4,1,8192]{4,2,1,0,3:T(4,128)(2,1)S(1)}, bf16[2,2,4,1,8192]{4,2,1,0,3:T(4,128)(2,1)S(1)}, u32[]{:S(2)}, u32[]{:S(2)}) collective-permute-start(bf16[2,2,4,1,8192]{4,2,1,0,3:T(4,128)(2,1)S(1)} %get-tuple-element.14), channel_id=1, source_target_pairs={{0,4},{1,5},{2,6},{3,7},{4,0},{5,1},{6,2},{7,3},{8,12},{9,13},{10,... | collective-permute-start | bytes 786440 | tf_op jit(solution)/shard_map/ppermute | solution.py:34
  158.0 18.3 %collective-permute-start.1 = (bf16[2,2,4,1,8192]{4,2,1,0,3:T(4,128)(2,1)S(1)}, bf16[2,2,4,1,8192]{4,2,1,0,3:T(4,128)(2,1)S(1)}, u32[]{:S(2)}, u32[]{:S(2)}) collective-permute-start(bf16[2,2,4,1,8192]{4,2,1,0,3:T(4,128)(2,1)S(1)} %get-tuple-element.16), channel_id=1, source_target_pairs={{0,2},{1,3},{2,0},{3,1},{4,6},{5,7},{6,4},{7,5},{8,10},{9,11},{10,... | collective-permute-start | bytes 786440 | tf_op jit(solution)/shard_map/ppermute | solution.py:34
  176.3 19.8 %collective-permute-start.2 = (bf16[2,2,4,1,8192]{4,2,1,0,3:T(4,128)(2,1)S(1)}, bf16[2,2,4,1,8192]{4,2,1,0,3:T(4,128)(2,1)S(1)}, u32[]{:S(2)}, u32[]{:S(2)}) collective-permute-start(bf16[2,2,4,1,8192]{4,2,1,0,3:T(4,128)(2,1)S(1)} %get-tuple-element.15), channel_id=1, source_target_pairs={{0,3},{1,2},{2,1},{3,0},{4,7},{5,6},{6,5},{7,4},{8,11},{9,10},{10,... | collective-permute-start | bytes 786440 | tf_op jit(solution)/shard_map/ppermute | solution.py:34
  196.7 1.3 copy-start.2
  254.8 51.7 %all-to-all-start.2 = ((bf16[8,2,1,8,8192]{4,1,0,2,3:T(2,128)(2,1)}), bf16[8,2,1,8,8192]{4,1,0,2,3:T(2,128)(2,1)S(1)}, u32[]{:S(2)}, u32[]{:S(2)}) async-start(bf16[8,2,1,8,8192]{4,1,0,2,3:T(2,128)(2,1)} %copy.39), calls=%async_computation.3 | async-start | bytes 4194304 | tf_op jit(solution)/shard_map/all_to_all | solution.py:132
Sparse Core Ops, SparseCore 0:
  12.7 47.2 reduce-scatter.1
